TPU v7x, 256 devices: a whole 4x4x8 slice. The times are simulated.
256 devices in a mesh: dp: 2 (over z_lo), expert: 32 (over y, z_hi, core), tensor: 4 (over x).
Axes of the slice: x: 4, y: 4, z: 8 (z_hi: 4, z_lo: 2; z = z_hi * 2 + z_lo), core: 2. Of those that a mesh axis runs over, the one named last changes fastest.
Arguments:
- context: bfloat16 [8192, 2048], P(('dp', 'expert'), 'tensor'), may hold values from -6 to 6
- residual: bfloat16 [8192, 2048], P(('dp', 'expert')), may hold values from -6 to 6
- wo_rows: bfloat16 [2048, 2048], P('tensor'), may hold values from -0.125 to 0.125
- norm_gain: float32 [2048], replicated, may hold values from 0.25 to 1.75
- analyzer_out: bfloat16 [8192, 2048], P(('dp', 'expert'), 'tensor'), may hold values from -6 to 6
- gate_probs: float32 [8192, 6], P(('dp', 'expert')), may hold values from 0.05 to 0.5
- expert_ids: int32 [8192, 6], P(('dp', 'expert')), may hold values from 0 to 63, all different within a row; in each aligned block of 128 rows (0 to 127, 128 to 255, ...) at most 14 rows name the same one
- w_gate_up: bfloat16 [64, 2, 2048, 1408], P('expert', None, 'dp', 'tensor'), may hold values from -0.125 to 0.125
- w_down: bfloat16 [64, 1408, 2048], P('expert', 'tensor', 'dp'), may hold values from -0.15625 to 0.15625
Outputs:
- block_out: bfloat16 [8192, 2048], P(('dp', 'expert'), 'tensor')
- context_grad: bfloat16 [8192, 2048], P(('dp', 'expert'), 'tensor')
- gate_prob_grad: float32 [8192, 6], P(('dp', 'expert'))
- gate_up_grad: bfloat16 [64, 2, 2048, 1408], P('expert', None, 'dp', 'tensor')
- down_grad: bfloat16 [64, 1408, 2048], P('expert', 'tensor', 'dp')
Inputs may be any that keep to these rules, and one draw needn't show every extreme that they name: `expert_ids`: each row names 6 different experts; within each device's rows (aligned blocks of 128 rows) no expert is named more than 14 times, a bound that some block reaches.
All inputs are finite; a program needn't handle non-finite values.
Results may differ from a plain program's by a relative error of at most 0.024.
Values may be sent and summed in bfloat16 or wider, within the bound.
No kernel may reach another device: no remote copies, remote signals or barrier semaphores. Data moves between devices by JAX's collectives and lax.ppermute only.
A program may use at most 128 MiB of HBM per device.

v0:
```python
import jax
import jax.numpy as jnp
from jax import lax
from jax.sharding import PartitionSpec as P

EXPERTS = 64
CAP = 14
NORM_EPS = 1e-06
LOSS_WEIGHT = 0.25


def to_experts(outgoing):
    return lax.all_to_all(outgoing, "expert", split_axis=1, concat_axis=1, tiled=True)


def to_tokens(outgoing):
    return lax.all_to_all(outgoing, "expert", split_axis=1, concat_axis=1, tiled=True)


def weight_terms(arrived, activation, grad_in, d_gate_pre, d_up_pre):
    down_part = jnp.einsum(
        "escf,escd->efd", activation, grad_in, preferred_element_type=jnp.float32
    )
    gate_part = jnp.einsum(
        "escd,escf->edf", arrived, d_gate_pre, preferred_element_type=jnp.float32
    )
    up_part = jnp.einsum("escd,escf->edf", arrived, d_up_pre, preferred_element_type=jnp.float32)
    return (jnp.stack([gate_part, up_part], axis=1), down_part)


def per_device(
    context, residual, wo_rows, norm_gain, analyzer_out, gate_probs, expert_ids, w_gate_up, w_down
):
    tok_count, top_count = expert_ids.shape
    feature_count = residual.shape[1]
    tensor_count = lax.axis_size("tensor")
    expert_ranks = lax.axis_size("expert")
    col_count = feature_count // tensor_count
    col_start = lax.axis_index("tensor") * col_count
    local_experts = w_gate_up.shape[0]
    slot_count = EXPERTS * CAP
    expert_range = jnp.arange(EXPERTS, dtype=jnp.int32)
    slot_order = expert_range % local_experts * expert_ranks + expert_range // local_experts
    gate_up_full, down_full = (
        lax.all_gather(w_gate_up, "dp", axis=2, tiled=True),
        lax.all_gather(w_down, "dp", axis=2, tiled=True),
    )
    partial_attn = jnp.dot(context, wo_rows, preferred_element_type=jnp.float32)
    hidden_in = residual.astype(jnp.float32) + lax.psum(
        partial_attn.astype(jnp.bfloat16), "tensor"
    ).astype(jnp.float32)
    inv_rms = lax.rsqrt(jnp.mean(hidden_in * hidden_in, axis=1, keepdims=True) + NORM_EPS)
    normed = (norm_gain * hidden_in * inv_rms).astype(jnp.bfloat16)
    flat_ids = expert_ids.reshape(-1)
    onehot = (flat_ids[:, None] == expert_range[None, :]).astype(jnp.int32)
    slot_index = jnp.sum((jnp.cumsum(onehot, axis=0) - onehot) * onehot, axis=1)
    expert_slot = jnp.sum(onehot * slot_order[None, :], axis=1)
    dest_row = expert_slot * CAP + slot_index
    sentinel = tok_count * top_count
    row_entry = (
        jnp.full((slot_count,), sentinel, jnp.int32)
        .at[dest_row]
        .set(jnp.arange(sentinel, dtype=jnp.int32))
    )
    row_token = row_entry // top_count
    gate_pad = jnp.concatenate([gate_probs.reshape(-1), jnp.zeros((1,), jnp.float32)])
    row_gate = gate_pad[row_entry]
    normed_pad = jnp.concatenate([normed, jnp.zeros((1, feature_count), jnp.bfloat16)], axis=0)
    outgoing = normed_pad[row_token].reshape(local_experts, expert_ranks, CAP, feature_count)
    arrived = to_experts(outgoing)
    gate_full = gate_up_full[:, 0]
    up_full = gate_up_full[:, 1]
    pre_gate = jnp.einsum("escd,edf->escf", arrived, gate_full, preferred_element_type=jnp.float32)
    pre_up = jnp.einsum("escd,edf->escf", arrived, up_full, preferred_element_type=jnp.float32)
    activation = (jax.nn.silu(pre_gate) * pre_up).astype(jnp.bfloat16)
    partial_out = jnp.einsum(
        "escf,efd->escd", activation, down_full, preferred_element_type=jnp.float32
    )
    summed_out = lax.psum_scatter(
        partial_out.astype(jnp.bfloat16), "tensor", scatter_dimension=3, tiled=True
    )
    returned = to_tokens(summed_out).reshape(slot_count, col_count)
    entry_out = returned[dest_row].reshape(tok_count, top_count, col_count).astype(jnp.float32)
    hidden_cols = lax.dynamic_slice_in_dim(hidden_in, col_start, col_count, 1)
    block_out = (hidden_cols + jnp.sum(gate_probs[:, :, None] * entry_out, axis=1)).astype(
        jnp.bfloat16
    )
    error = (
        LOSS_WEIGHT * (block_out.astype(jnp.float32) - analyzer_out.astype(jnp.float32))
    ).astype(jnp.bfloat16)
    gate_partial = jnp.sum(error.astype(jnp.float32)[:, None, :] * entry_out, axis=2)
    error_full = lax.all_gather(error, "tensor", axis=1, tiled=True)
    error_pad = jnp.concatenate([error_full, jnp.zeros((1, feature_count), jnp.bfloat16)], axis=0)
    grad_slot = (row_gate[:, None] * error_pad[row_token].astype(jnp.float32)).astype(jnp.bfloat16)
    grad_slot = grad_slot.reshape(local_experts, expert_ranks, CAP, feature_count)
    grad_in = to_experts(grad_slot)
    d_act = jnp.einsum("escd,efd->escf", grad_in, down_full, preferred_element_type=jnp.float32)
    sigmoid_pre = jax.nn.sigmoid(pre_gate)
    d_gate_pre = (d_act * pre_up * sigmoid_pre * (1.0 + pre_gate * (1.0 - sigmoid_pre))).astype(
        jnp.bfloat16
    )
    d_up_pre = (d_act * pre_gate * sigmoid_pre).astype(jnp.bfloat16)
    d_entry_part = jnp.einsum(
        "escf,edf->escd", d_gate_pre, gate_full, preferred_element_type=jnp.float32
    )
    d_entry_part = d_entry_part + jnp.einsum(
        "escf,edf->escd", d_up_pre, up_full, preferred_element_type=jnp.float32
    )
    d_entry_sum = lax.psum_scatter(
        d_entry_part.astype(jnp.bfloat16), "tensor", scatter_dimension=3, tiled=True
    )
    d_returned = to_tokens(d_entry_sum).reshape(slot_count, col_count)
    d_normed = jnp.sum(
        d_returned[dest_row].reshape(tok_count, top_count, col_count).astype(jnp.float32), axis=1
    )
    gain_cols = lax.dynamic_slice_in_dim(norm_gain, col_start, col_count, 0)
    scaled = gain_cols * d_normed
    norm_partial = jnp.sum(scaled * hidden_cols, axis=1)
    norm_dots, gate_prob_grad = lax.psum((norm_partial, gate_partial), "tensor")
    cubed = inv_rms * inv_rms * inv_rms
    d_hidden = (
        error.astype(jnp.float32)
        + inv_rms * scaled
        - hidden_cols * cubed * norm_dots[:, None] / feature_count
    ).astype(jnp.bfloat16)
    context_grad = lax.dot_general(
        lax.all_gather(d_hidden, "tensor", axis=1, tiled=True),
        wo_rows,
        (((1,), (1,)), ((), ())),
        preferred_element_type=jnp.float32,
    ).astype(jnp.bfloat16)
    gate_up_part, down_part = weight_terms(arrived, activation, grad_in, d_gate_pre, d_up_pre)
    gate_up_grad, down_grad = (
        lax.psum_scatter(
            gate_up_part.astype(jnp.bfloat16), "dp", scatter_dimension=2, tiled=True
        ).astype(jnp.float32),
        lax.psum_scatter(
            down_part.astype(jnp.bfloat16), "dp", scatter_dimension=2, tiled=True
        ).astype(jnp.float32),
    )
    return (
        block_out,
        context_grad,
        gate_prob_grad,
        gate_up_grad.astype(jnp.bfloat16),
        down_grad.astype(jnp.bfloat16),
    )


def solution(mesh):
    in_specs = (
        P(("dp", "expert"), "tensor"),
        P(("dp", "expert"), None),
        P("tensor", None),
        P(),
        P(("dp", "expert"), "tensor"),
        P(("dp", "expert"), None),
        P(("dp", "expert"), None),
        P("expert", None, "dp", "tensor"),
        P("expert", "tensor", "dp"),
    )
    out_specs = (
        P(("dp", "expert"), "tensor"),
        P(("dp", "expert"), "tensor"),
        P(("dp", "expert"), None),
        P("expert", None, "dp", "tensor"),
        P("expert", "tensor", "dp"),
    )
    return jax.shard_map(
        per_device, mesh=mesh, in_specs=in_specs, out_specs=out_specs, check_vma=False
    )
```

profile of v0, /device:TPU:1, one launch (start us, length us, event | category | flops | bytes accessed | tf_op | source)
XLA Modules:
  0.0 653.3 jit_solution(14605199587444355152)
XLA Ops:
  9.6 2.1 convolution_convert_fusion.1
  11.8 3.7 copy.54
  16.6 1.8 reduce-window.6
  18.9 3.4 scatter_custom_fusion
  22.3 39.6 %all-reduce.5.cloned.1.call-done = bf16[128,2048]{1,0:T(8,128)(2,1)} async-done(((bf16[128,2048]{1,0:T(8,128)(2,1)}), bf16[128,2048]{1,0:T(8,128)(2,1)}) %all-reduce.5.cloned.1.call-update) | async-done | bytes 524304 | tf_op jit(solution)/shard_map/psum | solution.py:49
  63.2 2.3 convert_add_fusion
  65.5 5.0 gather_fusion
  70.5 6.0 reshape.133
  76.5 7.8 %copy.53 = bf16[2,32,14,2048]{3,0,2,1:T(2,128)(2,1)} copy(bf16[2,32,14,2048]{3,2,1,0:T(8,128)(2,1)} %reshape.133) | data formatting | bytes 7340032 | tf_op jit(solution)/shard_map/reshape | solution.py:69
  84.3 12.4 %all-to-all-start = ((bf16[2,32,14,2048]{3,0,2,1:T(2,128)(2,1)}), bf16[2,32,14,2048]{3,0,2,1:T(2,128)(2,1)}, u32[]{:S(2)}, u32[]{:S(2)}) async-start(bf16[2,32,14,2048]{3,0,2,1:T(2,128)(2,1)} %copy.53), calls=%async_computation | async-start | bytes 7340032 | tf_op jit(solution)/shard_map/all_to_all | solution.py:13
  98.7 109.8 %all-to-all-done = bf16[2,32,14,2048]{3,0,2,1:T(2,128)(2,1)} async-done(((bf16[2,32,14,2048]{3,0,2,1:T(2,128)(2,1)}), bf16[2,32,14,2048]{3,0,2,1:T(2,128)(2,1)}, u32[]{:S(2)}, u32[]{:S(2)}) %all-to-all-start) | async-done | bytes 3670048 | tf_op jit(solution)/shard_map/all_to_all | solution.py:13
  208.5 7.4 %fusion.8 = f32[2,32,14,352]{3,1,2,0:T(8,128)S(1)} fusion(bf16[2,2,2048,352]{2,3,0,1:T(8,128)(2,1)} %all-gather.3.cloned.1.call-done, bf16[2,32,14,2048]{3,0,2,1:T(2,128)(2,1)} %all-to-all-done), kind=kOutput, calls=%fused_computation.23 | convolution fusion | flops 1291845632 | bytes 7815168 | tf_op jit(solution)/shard_map/escd,edf->escf/dot_general | solution.py:73
  217.1 7.7 %multiply_convert_fusion.3 = (bf16[2,32,14,352]{3,1,2,0:T(8,128)(2,1)S(1)}, f32[2,32,14,352]{3,1,2,0:T(8,128)}) fusion(f32[2,32,14,352]{3,1,2,0:T(8,128)S(1)} %fusion.8, bf16[2,2,2048,352]{2,3,0,1:T(8,128)(2,1)S(1)} %copy-done.1, bf16[2,32,14,2048]{3,0,2,1:T(2,128)(2,1)} %all-to-all-done), kind=kOutput, calls=%fused_computation.34 | convolution fusion | flops 1293737984 | bytes 9822208 | tf_op jit(solution)/shard_map/escd,edf->escf/dot_general | solution.py:74
  224.8 5.9 convolution_convert_fusion
  230.8 41.4 %reduce-scatter.5.cloned.1.call-done = bf16[2,32,14,512]{3,1,2,0:T(8,128)(2,1)} async-done(((bf16[2,32,14,2048]{3,1,2,0:T(8,128)(2,1)}), bf16[2,32,14,512]{3,1,2,0:T(8,128)(2,1)}) %reduce-scatter.5.cloned.1.call-update) | async-done | bytes 917520 | tf_op jit(solution)/shard_map/reduce_scatter | solution.py:79
  272.2 3.0 copy.57
  275.2 10.7 %all-to-all-start.1 = ((bf16[2,32,14,512]{3,0,2,1:T(2,128)(2,1)}), bf16[2,32,14,512]{3,0,2,1:T(2,128)(2,1)S(1)}, u32[]{:S(2)}, u32[]{:S(2)}) async-start(bf16[2,32,14,512]{3,0,2,1:T(2,128)(2,1)} %copy.57), calls=%async_computation.2 | async-start | bytes 1835008 | tf_op jit(solution)/shard_map/all_to_all | solution.py:17
  286.3 3.7 gather_fusion.2
  290.1 21.6 %all-to-all-done.1 = bf16[2,32,14,512]{3,0,2,1:T(2,128)(2,1)S(1)} async-done(((bf16[2,32,14,512]{3,0,2,1:T(2,128)(2,1)}), bf16[2,32,14,512]{3,0,2,1:T(2,128)(2,1)S(1)}, u32[]{:S(2)}, u32[]{:S(2)}) %all-to-all-start.1) | async-done | bytes 917536 | tf_op jit(solution)/shard_map/all_to_all | solution.py:17
  314.3 3.3 gather_fusion.1
  317.7 2.5 reshape.137
  320.2 2.3 multiply_reduce_fusion.1
  324.2 10.3 %all_gather.14 = bf16[128,2048]{1,0:T(8,128)(2,1)S(1)} all-gather(bf16[128,512]{1,0:T(8,128)(2,1)S(1)} %get-tuple-element.30), channel_id=1, replica_groups=mesh['dp'=2,'expert'=32,'tensor'=4] {'tensor'}, dimensions={1}, use_global_device_ids=true | all-gather | bytes 655360 | tf_op jit(solution)/shard_map/all_gather | solution.py:92
  334.5 5.0 gather_fusion.3
  339.5 6.3 reshape.138
  345.8 3.9 multiply_convert_fusion
  349.7 3.8 copy.60
  353.5 92.5 %all_to_all.20 = bf16[2,32,14,2048]{3,0,2,1:T(2,128)(2,1)S(1)} all-to-all(bf16[2,32,14,2048]{3,0,2,1:T(2,128)(2,1)S(1)} %copy.60), channel_id=1, replica_groups=mesh['dp'=2,'expert'=32,'tensor'=4] {'expert'}, dimensions={1} | all-to-all | bytes 7340032 | tf_op jit(solution)/shard_map/all_to_all | solution.py:13
  446.0 7.9 %multiply_convert_fusion.1 = (bf16[2,32,14,352]{3,1,2,0:T(8,128)(2,1)S(1)}, bf16[2,32,14,352]{3,1,2,0:T(8,128)(2,1)S(1)}) fusion(f32[2,32,14,352]{3,1,2,0:T(8,128)} %copy-done.14, f32[2,32,14,352]{3,1,2,0:T(8,128)} %get-tuple-element.41, bf16[2,352,2048]{2,1,0:T(8,128)(2,1)S(1)} %copy-done.4, bf16[2,32,14,2048]{3,0,2,1:T(2,128)(2,1)S(1)} %all_to_all.20), kind=kOutput, calls=%fused_computation.32 | convolution fusion | flops 1295945728 | bytes 10338304 | tf_op jit(solution)/shard_map/escd,efd->escf/dot_general | solution.py:97
  454.0 2.1 fusion.7
  456.0 4.0 add_convert_fusion
  460.3 6.8 %fusion.4 = bf16[2,1,2048,352]{2,3,0,1:T(8,128)(2,1)S(1)} fusion(bf16[2,32,14,352]{3,1,2,0:T(8,128)(2,1)S(1)} %get-tuple-element.32, bf16[2,32,14,2048]{3,0,2,1:T(2,128)(2,1)} %all-to-all-done), kind=kOutput, calls=%fused_computation.17 | convolution fusion | flops 1293287424 | bytes 7184384 | tf_op jit(solution)/shard_map/escd,escf->edf/dot_general | solution.py:27
  467.2 6.8 %fusion.3 = bf16[2,1,2048,352]{2,3,0,1:T(8,128)(2,1)S(1)} fusion(bf16[2,32,14,352]{3,1,2,0:T(8,128)(2,1)S(1)} %copy-done.9, bf16[2,32,14,2048]{3,0,2,1:T(2,128)(2,1)} %all-to-all-done), kind=kOutput, calls=%fused_computation.16 | convolution fusion | flops 1293287424 | bytes 7184384 | tf_op jit(solution)/shard_map/escd,escf->edf/dot_general | solution.py:24
  474.0 3.0 pad_maximum_fusion
  478.1 8.3 %bitcast_convert_fusion = bf16[2,352,2048]{2,1,0:T(8,128)(2,1)} fusion(bf16[2,32,14,352]{3,1,2,0:T(8,128)(2,1)S(1)} %copy-done.7, bf16[2,32,14,2048]{3,0,2,1:T(2,128)(2,1)} %copy-done.2), kind=kOutput, calls=%fused_computation.9 | convolution fusion | flops 1293287424 | bytes 7184384 | tf_op jit(solution)/shard_map/escf,escd->efd/dot_general | solution.py:21
  486.4 13.3 %reduce-scatter.7.cloned.1.call-done = bf16[2,32,14,512]{3,1,2,0:T(8,128)(2,1)} async-done(((bf16[2,32,14,2048]{3,1,2,0:T(8,128)(2,1)}), bf16[2,32,14,512]{3,1,2,0:T(8,128)(2,1)}) %reduce-scatter.7.cloned.1.call-update) | async-done | bytes 917520 | tf_op jit(solution)/shard_map/reduce_scatter | solution.py:109
  499.7 3.1 copy.62
  502.8 10.3 %all-to-all-start.3 = ((bf16[2,32,14,512]{3,0,2,1:T(2,128)(2,1)}), bf16[2,32,14,512]{3,0,2,1:T(2,128)(2,1)S(1)}, u32[]{:S(2)}, u32[]{:S(2)}) async-start(bf16[2,32,14,512]{3,0,2,1:T(2,128)(2,1)} %copy.62), calls=%async_computation.5 | async-start | bytes 1835008 | tf_op jit(solution)/shard_map/all_to_all | solution.py:17
  513.2 3.0 multiply_reduce_fusion
  516.3 33.2 %all-to-all-done.3 = bf16[2,32,14,512]{3,0,2,1:T(2,128)(2,1)S(1)} async-done(((bf16[2,32,14,512]{3,0,2,1:T(2,128)(2,1)}), bf16[2,32,14,512]{3,0,2,1:T(2,128)(2,1)S(1)}, u32[]{:S(2)}, u32[]{:S(2)}) %all-to-all-start.3) | async-done | bytes 917536 | tf_op jit(solution)/shard_map/all_to_all | solution.py:17
  552.2 3.3 gather_fusion.4
  555.5 2.5 reshape.139
  558.1 2.5 reduce_sum.67
  560.7 12.6 %all-reduce.2 = (f32[128]{0:T(128)}, f32[128,6]{1,0:T(8,128)}) all-reduce(f32[128]{0:T(128)S(1)} %multiply_reduce_fusion.3, f32[128,6]{1,0:T(8,128)} %multiply_reduce_fusion), channel_id=1, replica_groups=mesh['dp'=2,'expert'=32,'tensor'=4] {'tensor'}, use_global_device_ids=true, to_apply=%region_12.13 | all-reduce | flops 896 | bytes 7168 | tf_op jit(solution)/shard_map/psum | solution.py:119
  575.6 10.6 %all_gather.15 = bf16[128,2048]{1,0:T(8,128)(2,1)S(1)} all-gather(bf16[128,512]{1,0:T(8,128)(2,1)S(1)} %subtract_convert_fusion), channel_id=1, replica_groups=mesh['dp'=2,'expert'=32,'tensor'=4] {'tensor'}, dimensions={1}, use_global_device_ids=true | all-gather | bytes 655360 | tf_op jit(solution)/shard_map/all_gather | solution.py:127
  587.8 10.1 %reduce-scatter.9.cloned.1.call-done = bf16[2,2,1024,352]{2,3,0,1:T(8,128)(2,1)} async-done(((bf16[2,2,2048,352]{2,3,0,1:T(8,128)(2,1)}), bf16[2,2,1024,352]{2,3,0,1:T(8,128)(2,1)}) %reduce-scatter.9.cloned.1.call-update) | async-done | bytes 2883600 | tf_op jit(solution)/shard_map/reduce_scatter | solution.py:134
  597.9 3.7 copy.68
  601.6 44.2 %reduce-scatter.11.cloned.1.call-done = bf16[2,352,1024]{2,1,0:T(8,128)(2,1)} async-done(((bf16[2,352,2048]{2,1,0:T(8,128)(2,1)}), bf16[2,352,1024]{2,1,0:T(8,128)(2,1)}) %reduce-scatter.11.cloned.1.call-update) | async-done | bytes 1441808 | tf_op jit(solution)/shard_map/reduce_scatter | solution.py:137
  (83 shorter events, 20.4 us)
Async XLA Ops:
  8.0 1.6 copy-start
  8.0 53.9 %all-reduce.5.cloned.1.call-start = ((), (), s32[]{:S(2)}) async-start(), calls=%async_computation.8 | async-start | bytes 1048576 | tf_op jit(solution)/shard_map/psum | solution.py:49
  11.8 86.9 %all-gather.3.cloned.1.call-start = ((), (), s32[]{:S(2)}) async-start(), calls=%async_computation.9 | async-start | bytes 8650752 | tf_op jit(solution)/shard_map/all_gather | solution.py:45
  15.5 0.7 copy-start.12
  15.5 46.4 %copy-start.5 = (bf16[128,2048]{1,0:T(8,128)(2,1)S(1)}, bf16[128,2048]{1,0:T(8,128)(2,1)}, u32[]{:S(2)}) copy-start(bf16[128,2048]{1,0:T(8,128)(2,1)} %param.10) | copy-start | bytes 1572868
  15.5 47.7 %copy-start.11 = (f32[2048]{0:T(1024)S(1)}, f32[2048]{0:T(1024)}, u32[]{:S(2)}) copy-start(f32[2048]{0:T(1024)} %param.12) | copy-start | bytes 24580
  84.3 124.2 %all-to-all-start = ((bf16[2,32,14,2048]{3,0,2,1:T(2,128)(2,1)}), bf16[2,32,14,2048]{3,0,2,1:T(2,128)(2,1)}, u32[]{:S(2)}, u32[]{:S(2)}) async-start(bf16[2,32,14,2048]{3,0,2,1:T(2,128)(2,1)} %copy.53), calls=%async_computation | async-start | bytes 7340032 | tf_op jit(solution)/shard_map/all_to_all | solution.py:13
  96.8 128.1 %all-gather.5.cloned.1.call-start = ((), (), s32[]{:S(2)}) async-start(), calls=%async_computation.10 | async-start | bytes 4325376 | tf_op jit(solution)/shard_map/all_gather | solution.py:46
  97.3 174.9 %reduce-scatter.5.cloned.1.call-start = ((), (), s32[]{:S(2)}) async-start(), calls=%async_computation.11 | async-start | bytes 4587520 | tf_op jit(solution)/shard_map/reduce_scatter | solution.py:79
  208.5 8.6 %copy-start.1 = (bf16[2,2,2048,352]{2,3,0,1:T(8,128)(2,1)S(1)}, bf16[2,2,2048,352]{2,3,0,1:T(8,128)(2,1)}, u32[]{:S(2)}) copy-start(bf16[2,2,2048,352]{2,3,0,1:T(8,128)(2,1)} %all-gather.3.cloned.1.call-done) | copy-start | bytes 17301508
  215.9 1.2 copy-start.14
  224.8 5.9 copy-start.6
  230.8 55.3 %copy-start.13 = (f32[128,6]{0,1:T(8,128)S(1)}, f32[128,6]{0,1:T(8,128)}, u32[]{:S(2)}) copy-start(f32[128,6]{0,1:T(8,128)} %param.14) | copy-start | bytes 9220
  275.2 36.5 %all-to-all-start.1 = ((bf16[2,32,14,512]{3,0,2,1:T(2,128)(2,1)}), bf16[2,32,14,512]{3,0,2,1:T(2,128)(2,1)S(1)}, u32[]{:S(2)}, u32[]{:S(2)}) async-start(bf16[2,32,14,512]{3,0,2,1:T(2,128)(2,1)} %copy.57), calls=%async_computation.2 | async-start | bytes 1835008 | tf_op jit(solution)/shard_map/all_to_all | solution.py:17
  286.0 213.7 %reduce-scatter.7.cloned.1.call-start = ((), (), s32[]{:S(2)}) async-start(), calls=%async_computation.12 | async-start | bytes 4587520 | tf_op jit(solution)/shard_map/reduce_scatter | solution.py:109
  317.7 4.8 copy-start.10
  353.5 92.5 %copy-start.4 = (bf16[2,352,2048]{2,1,0:T(8,128)(2,1)S(1)}, bf16[2,352,2048]{2,1,0:T(8,128)(2,1)}, u32[]{:S(2)}) copy-start(bf16[2,352,2048]{2,1,0:T(8,128)(2,1)} %all-gather.5.cloned.1.call-done) | copy-start | bytes 8650756
  353.5 100.4 %slice-start = ((s8[5767168]{0:T(1024)(128)(4,1)}), s8[4194304]{0:T(1024)(128)(4,1)S(1)}, s32[]{:S(2)}) async-start(s8[5767168]{0:T(1024)(128)(4,1)} %bitcast.73), calls=%async_computation.15 | async-start | bytes 8388608
  446.0 7.9 %copy-start.2 = (bf16[2,32,14,2048]{3,0,2,1:T(2,128)(2,1)}, bf16[2,32,14,2048]{3,0,2,1:T(2,128)(2,1)S(1)}, u32[]{:S(2)}) copy-start(bf16[2,32,14,2048]{3,0,2,1:T(2,128)(2,1)S(1)} %all_to_all.20) | copy-start | bytes 11010052
  446.0 7.9 %slice-start.1 = ((s8[5767168]{0:T(1024)(128)(4,1)}), s8[1572864]{0:T(1024)(128)(4,1)S(1)}, s32[]{:S(2)}) async-start(s8[5767168]{0:T(1024)(128)(4,1)} %bitcast.73), calls=%async_computation.16 | async-start | bytes 3145728
  453.9 2.1 copy-start.8
  460.1 137.8 %reduce-scatter.9.cloned.1.call-start = ((), (), s32[]{:S(2)}) async-start(), calls=%async_computation.13 | async-start | bytes 8650752 | tf_op jit(solution)/shard_map/reduce_scatter | solution.py:134
  460.3 6.8 %copy-start.9 = (bf16[2,32,14,352]{3,1,2,0:T(8,128)(2,1)S(1)}, bf16[2,32,14,352]{3,1,2,0:T(8,128)(2,1)}, u32[]{:S(2)}) copy-start(bf16[2,32,14,352]{3,1,2,0:T(8,128)(2,1)} %copy-done.8) | copy-start | bytes 1892356
  476.9 1.1 copy-start.7
  477.0 168.7 %reduce-scatter.11.cloned.1.call-start = ((), (), s32[]{:S(2)}) async-start(), calls=%async_computation.14 | async-start | bytes 4325376 | tf_op jit(solution)/shard_map/reduce_scatter | solution.py:137
  502.8 46.7 %all-to-all-start.3 = ((bf16[2,32,14,512]{3,0,2,1:T(2,128)(2,1)}), bf16[2,32,14,512]{3,0,2,1:T(2,128)(2,1)S(1)}, u32[]{:S(2)}, u32[]{:S(2)}) async-start(bf16[2,32,14,512]{3,0,2,1:T(2,128)(2,1)} %copy.62), calls=%async_computation.5 | async-start | bytes 1835008 | tf_op jit(solution)/shard_map/all_to_all | solution.py:17
  555.5 5.0 copy-start.3
Sparse Core Ops, SparseCore 0:
  11.9 49.9 all-reduce.4
  230.9 41.2 reduce-scatter.4
  460.2 39.4 reduce-scatter.6
  502.1 95.7 reduce-scatter.8
  600.8 44.8 reduce-scatter.10
Sparse Core Ops, SparseCore 1:
  15.6 83.0 all-gather.2
  100.3 108.2 all-gather.4
where the time goes:
time: 661 us; the launch traced here: 653 us
  waiting for transfers between devices  315 us (48%)
  blocking collectives  126 us (19%)
  local copies, waits for them, and re-layouts  78.2 us (12%)
  matrix products  60.6 us (9%)
  starting transfers between devices  34.5 us (5%)
  other arithmetic  22.9 us (3%)
  between operations  16.1 us (2%)
    all_to_all x1, waiting for transfers between devices, to_experts(): lax.all_to_all(outgoing, 'expert', split_axis=1, concat_axis=1, tiled=True)  110 us
    all_to_all x1, blocking collectives, to_experts(): lax.all_to_all(outgoing, 'expert', split_axis=1, concat_axis=1, tiled=True)  92.5 us
    all_to_all x2, waiting for transfers between devices, to_tokens(): lax.all_to_all(outgoing, 'expert', split_axis=1, concat_axis=1, tiled=True)  54.9 us
    reduce_scatter x1, waiting for transfers between devices, per_device(): lax.psum_scatter(down_part.astype(jnp.bfloat16), 'dp', scatter_dimension=...  44.2 us
    reduce_scatter x1, waiting for transfers between devices, per_device(): lax.psum_scatter(partial_out.astype(jnp.bfloat16), 'tensor', scatter_dime...  41.4 us
    psum x1, waiting for transfers between devices, per_device(): lax.psum(partial_attn.astype(jnp.bfloat16), 'tensor').astype(jnp.float32)  39.6 us
    all_to_all x2, starting transfers between devices, to_tokens(): lax.all_to_all(outgoing, 'expert', split_axis=1, concat_axis=1, tiled=True)  21.1 us
    reshape x2, local copies, waits for them, and re-layouts, per_device(): normed_pad[row_token]  13.8 us
  transfers between devices with their start and end apart: 10, of which 9 were waited for; matrix products, arithmetic and copies ran while one was open for 15% of the time, Pallas kernels for 0%

commit v1 on v0

--- a/solution.py
+++ b/solution.py
@@ -14,7 +14,12 @@
 
 
 def to_tokens(outgoing):
-    return lax.all_to_all(outgoing, "expert", split_axis=1, concat_axis=1, tiled=True)
+    return jnp.concatenate(
+        lax.all_to_all(
+            jnp.stack(jnp.split(outgoing, lax.axis_size("expert"), axis=1)), "expert", 0, 0
+        ),
+        axis=1,
+    )
 
 
 def weight_terms(arrived, activation, grad_in, d_gate_pre, d_up_pre):

time: 661 us -> 670 us (1.014)
    split x0 -> x66, local copies, waits for them, and re-layouts: none -> 10.5 us  [to_tokens(): jnp.split(outgoing, lax.axis_size('expert'), axis=1)]
  transfers between devices with their start and end apart: 10 -> 10, of which waited for: 9 -> 8; matrix products, arithmetic and copies ran while one was open for 15% -> 15% of each run, Pallas kernels for 0% -> 0%
where the time goes in v1:
time: 670 us; the launch traced here: 662 us
  waiting for transfers between devices  318 us (47%)
  blocking collectives  127 us (19%)
  local copies, waits for them, and re-layouts  82.5 us (12%)
  matrix products  60.6 us (9%)
  starting transfers between devices  34.1 us (5%)
  other arithmetic  22.2 us (3%)
  between operations  17.1 us (3%)
    all_to_all x1, waiting for transfers between devices, to_experts(): lax.all_to_all(outgoing, 'expert', split_axis=1, concat_axis=1, tiled=True)  116 us
    all_to_all x1, blocking collectives, to_experts(): lax.all_to_all(outgoing, 'expert', split_axis=1, concat_axis=1, tiled=True)  92.3 us
    all_to_all x2, waiting for transfers between devices, to_tokens(): lax.all_to_all(jnp.stack(jnp.split(outgoing, lax.axis_size('expert'), axi...  55.7 us
    reduce_scatter x1, waiting for transfers between devices, per_device(): lax.psum_scatter(down_part.astype(jnp.bfloat16), 'dp', scatter_dimension=...  45.4 us
    psum x1, waiting for transfers between devices, per_device(): lax.psum(partial_attn.astype(jnp.bfloat16), 'tensor').astype(jnp.float32)  43.3 us
    reduce_scatter x1, waiting for transfers between devices, per_device(): lax.psum_scatter(partial_out.astype(jnp.bfloat16), 'tensor', scatter_dime...  39.2 us
    all_to_all x2, starting transfers between devices, to_tokens(): lax.all_to_all(jnp.stack(jnp.split(outgoing, lax.axis_size('expert'), axi...  20.7 us
    psum x1, blocking collectives, per_device(): norm_dots, gate_prob_grad = lax.psum((norm_partial, gate_partial), 'tensor')  14 us
  transfers between devices with their start and end apart: 10, of which 8 were waited for; matrix products, arithmetic and copies ran while one was open for 15% of the time, Pallas kernels for 0%

profile of v1, /device:TPU:1, one launch (start us, length us, event | category | flops | bytes accessed | tf_op | source)
XLA Modules:
  0.0 661.7 jit_solution(12023215521845631480)
XLA Ops:
  9.6 2.1 convolution_convert_fusion.1
  15.1 3.4 scatter_custom_fusion
  18.5 43.3 %all-reduce.5.cloned.1.call-done = bf16[128,2048]{1,0:T(8,128)(2,1)} async-done(((bf16[128,2048]{1,0:T(8,128)(2,1)}), bf16[128,2048]{1,0:T(8,128)(2,1)}) %all-reduce.5.cloned.1.call-update) | async-done | bytes 524304 | tf_op jit(solution)/shard_map/psum | solution.py:54
  63.1 2.2 convert_add_fusion
  65.4 5.0 gather_fusion
  70.4 6.0 reshape.133
  76.4 7.8 %copy.3511 = bf16[2,32,14,2048]{3,0,2,1:T(2,128)(2,1)} copy(bf16[2,32,14,2048]{3,2,1,0:T(8,128)(2,1)} %reshape.133) | data formatting | bytes 7340032 | tf_op jit(solution)/shard_map/reshape | solution.py:74
  84.2 12.4 %all-to-all-start = ((bf16[2,32,14,2048]{3,0,2,1:T(2,128)(2,1)}), bf16[2,32,14,2048]{3,0,2,1:T(2,128)(2,1)}, u32[]{:S(2)}, u32[]{:S(2)}) async-start(bf16[2,32,14,2048]{3,0,2,1:T(2,128)(2,1)} %copy.3511), calls=%async_computation | async-start | bytes 7340032 | tf_op jit(solution)/shard_map/all_to_all | solution.py:13
  97.5 115.6 %all-to-all-done = bf16[2,32,14,2048]{3,0,2,1:T(2,128)(2,1)} async-done(((bf16[2,32,14,2048]{3,0,2,1:T(2,128)(2,1)}), bf16[2,32,14,2048]{3,0,2,1:T(2,128)(2,1)}, u32[]{:S(2)}, u32[]{:S(2)}) %all-to-all-start) | async-done | bytes 3670048 | tf_op jit(solution)/shard_map/all_to_all | solution.py:13
  213.1 7.4 %fusion.8 = f32[2,32,14,352]{3,1,2,0:T(8,128)S(1)} fusion(bf16[2,2,2048,352]{2,3,1,0:T(8,128)(2,1)} %all-gather.3.cloned.1.call-done, bf16[2,32,14,2048]{3,0,2,1:T(2,128)(2,1)} %all-to-all-done), kind=kOutput, calls=%fused_computation.23 | convolution fusion | flops 1291845632 | bytes 7815168 | tf_op jit(solution)/shard_map/escd,edf->escf/dot_general | solution.py:78
  221.8 7.7 %multiply_convert_fusion.3 = (bf16[2,32,14,352]{3,1,2,0:T(8,128)(2,1)S(1)}, f32[2,32,14,352]{3,1,2,0:T(8,128)}) fusion(f32[2,32,14,352]{3,1,2,0:T(8,128)S(1)} %fusion.8, bf16[2,2,2048,352]{2,3,1,0:T(8,128)(2,1)S(1)} %copy-done.1, bf16[2,32,14,2048]{3,0,2,1:T(2,128)(2,1)} %all-to-all-done), kind=kOutput, calls=%fused_computation.34 | convolution fusion | flops 1293737984 | bytes 9822208 | tf_op jit(solution)/shard_map/escd,edf->escf/dot_general | solution.py:79
  229.5 5.9 convolution_convert_fusion
  235.5 39.2 %reduce-scatter.5.cloned.1.call-done = bf16[2,32,14,512]{3,1,2,0:T(8,128)(2,1)} async-done(((bf16[2,32,14,2048]{3,1,2,0:T(8,128)(2,1)}), bf16[2,32,14,512]{3,1,2,0:T(8,128)(2,1)}) %reduce-scatter.5.cloned.1.call-update) | async-done | bytes 917520 | tf_op jit(solution)/shard_map/reduce_scatter | solution.py:84
  274.6 3.2 fusion.28
  280.9 1.9 copy.3576
  282.8 10.4 %all-to-all-start.1 = ((bf16[32,2,1,14,512]{4,1,3,2,0:T(2,128)(2,1)}), bf16[32,2,1,14,512]{4,1,3,2,0:T(2,128)(2,1)S(1)}, u32[]{:S(2)}, u32[]{:S(2)}) async-start(bf16[32,2,1,14,512]{4,1,3,2,0:T(2,128)(2,1)} %copy.3576), calls=%async_computation.2 | async-start | bytes 1835008 | tf_op jit(solution)/shard_map/all_to_all | solution.py:18
  293.4 3.7 gather_fusion.2
  297.3 21.6 %all-to-all-done.1 = bf16[32,2,1,14,512]{4,1,3,2,0:T(2,128)(2,1)S(1)} async-done(((bf16[32,2,1,14,512]{4,1,3,2,0:T(2,128)(2,1)}), bf16[32,2,1,14,512]{4,1,3,2,0:T(2,128)(2,1)S(1)}, u32[]{:S(2)}, u32[]{:S(2)}) %all-to-all-start.1) | async-done | bytes 917536 | tf_op jit(solution)/shard_map/all_to_all | solution.py:18
  321.5 3.3 gather_fusion.1
  324.8 2.5 reshape.137
  327.3 2.3 multiply_reduce_fusion.1
  331.3 10.3 %all_gather.14 = bf16[128,2048]{1,0:T(8,128)(2,1)S(1)} all-gather(bf16[128,512]{1,0:T(8,128)(2,1)S(1)} %get-tuple-element.180), channel_id=1, replica_groups=mesh['dp'=2,'expert'=32,'tensor'=4] {'tensor'}, dimensions={1}, use_global_device_ids=true | all-gather | bytes 655360 | tf_op jit(solution)/shard_map/all_gather | solution.py:97
  341.6 5.0 gather_fusion.3
  346.7 6.3 reshape.138
  353.0 3.9 multiply_convert_fusion
  356.9 3.8 copy.3579
  360.7 92.3 %all_to_all.20 = bf16[2,32,14,2048]{3,0,2,1:T(2,128)(2,1)S(1)} all-to-all(bf16[2,32,14,2048]{3,0,2,1:T(2,128)(2,1)S(1)} %copy.3579), channel_id=1, replica_groups=mesh['dp'=2,'expert'=32,'tensor'=4] {'expert'}, dimensions={1} | all-to-all | bytes 7340032 | tf_op jit(solution)/shard_map/all_to_all | solution.py:13
  453.0 7.9 %multiply_convert_fusion.1 = (bf16[2,32,14,352]{3,1,2,0:T(8,128)(2,1)S(1)}, bf16[2,32,14,352]{3,1,2,0:T(8,128)(2,1)S(1)}) fusion(f32[2,32,14,352]{3,1,2,0:T(8,128)} %copy-done.16, f32[2,32,14,352]{3,1,2,0:T(8,128)} %get-tuple-element.255, bf16[2,352,2048]{2,1,0:T(8,128)(2,1)S(1)} %copy-done.6, bf16[2,32,14,2048]{3,0,2,1:T(2,128)(2,1)S(1)} %all_to_all.20), kind=kOutput, calls=%fused_computation.32 | convolution fusion | flops 1295945728 | bytes 10338304 | tf_op jit(solution)/shard_map/escd,efd->escf/dot_general | solution.py:102
  461.0 2.1 fusion.7
  463.1 4.0 add_convert_fusion
  467.4 6.8 %fusion.4 = bf16[2,1,2048,352]{2,3,0,1:T(8,128)(2,1)S(1)} fusion(bf16[2,32,14,352]{3,1,2,0:T(8,128)(2,1)S(1)} %get-tuple-element.182, bf16[2,32,14,2048]{3,0,2,1:T(2,128)(2,1)} %all-to-all-done), kind=kOutput, calls=%fused_computation.17 | convolution fusion | flops 1293287424 | bytes 7184384 | tf_op jit(solution)/shard_map/escd,escf->edf/dot_general | solution.py:32
  474.2 6.8 %fusion.3 = bf16[2,1,2048,352]{2,3,0,1:T(8,128)(2,1)S(1)} fusion(bf16[2,32,14,352]{3,1,2,0:T(8,128)(2,1)S(1)} %copy-done.11, bf16[2,32,14,2048]{3,0,2,1:T(2,128)(2,1)} %all-to-all-done), kind=kOutput, calls=%fused_computation.16 | convolution fusion | flops 1293287424 | bytes 7184384 | tf_op jit(solution)/shard_map/escd,escf->edf/dot_general | solution.py:29
  481.0 3.0 pad_maximum_fusion
  485.1 8.3 %bitcast_convert_fusion = bf16[2,352,2048]{2,1,0:T(8,128)(2,1)} fusion(bf16[2,32,14,352]{3,1,2,0:T(8,128)(2,1)S(1)} %copy-done.9, bf16[2,32,14,2048]{3,0,2,1:T(2,128)(2,1)} %copy-done.2), kind=kOutput, calls=%fused_computation.9 | convolution fusion | flops 1293287424 | bytes 7184384 | tf_op jit(solution)/shard_map/escf,escd->efd/dot_general | solution.py:26
  493.5 13.3 %reduce-scatter.7.cloned.1.call-done = bf16[2,32,14,512]{3,1,2,0:T(8,128)(2,1)} async-done(((bf16[2,32,14,2048]{3,1,2,0:T(8,128)(2,1)}), bf16[2,32,14,512]{3,1,2,0:T(8,128)(2,1)}) %reduce-scatter.7.cloned.1.call-update) | async-done | bytes 917520 | tf_op jit(solution)/shard_map/reduce_scatter | solution.py:114
  506.7 3.2 fusion.26
  512.5 1.9 copy.3643
  514.4 10.3 %all-to-all-start.3 = ((bf16[32,2,1,14,512]{4,1,3,2,0:T(2,128)(2,1)}), bf16[32,2,1,14,512]{4,1,3,2,0:T(2,128)(2,1)S(1)}, u32[]{:S(2)}, u32[]{:S(2)}) async-start(bf16[32,2,1,14,512]{4,1,3,2,0:T(2,128)(2,1)} %copy.3643), calls=%async_computation.5 | async-start | bytes 1835008 | tf_op jit(solution)/shard_map/all_to_all | solution.py:18
  524.9 2.6 multiply_reduce_fusion
  527.4 34.1 %all-to-all-done.3 = bf16[32,2,1,14,512]{4,1,3,2,0:T(2,128)(2,1)S(1)} async-done(((bf16[32,2,1,14,512]{4,1,3,2,0:T(2,128)(2,1)}), bf16[32,2,1,14,512]{4,1,3,2,0:T(2,128)(2,1)S(1)}, u32[]{:S(2)}, u32[]{:S(2)}) %all-to-all-start.3) | async-done | bytes 917536 | tf_op jit(solution)/shard_map/all_to_all | solution.py:18
  564.1 3.3 gather_fusion.4
  567.4 2.6 reshape.139
  570.0 2.2 reduce_sum.67
  572.3 14.0 %all-reduce.2 = (f32[128]{0:T(128)}, f32[128,6]{1,0:T(8,128)}) all-reduce(f32[128]{0:T(128)S(1)} %multiply_reduce_fusion.3, f32[128,6]{1,0:T(8,128)} %multiply_reduce_fusion), channel_id=1, replica_groups=mesh['dp'=2,'expert'=32,'tensor'=4] {'tensor'}, use_global_device_ids=true, to_apply=%region_12.13 | all-reduce | flops 896 | bytes 7168 | tf_op jit(solution)/shard_map/psum | solution.py:124
  588.6 10.9 %all_gather.15 = bf16[128,2048]{1,0:T(8,128)(2,1)S(1)} all-gather(bf16[128,512]{1,0:T(8,128)(2,1)S(1)} %subtract_convert_fusion), channel_id=1, replica_groups=mesh['dp'=2,'expert'=32,'tensor'=4] {'tensor'}, dimensions={1}, use_global_device_ids=true | all-gather | bytes 655360 | tf_op jit(solution)/shard_map/all_gather | solution.py:132
  601.0 4.1 reduce-scatter.9.cloned.1.call-done
  605.1 3.7 copy.3649
  608.8 45.4 %reduce-scatter.11.cloned.1.call-done = bf16[2,352,1024]{2,1,0:T(8,128)(2,1)} async-done(((bf16[2,352,2048]{2,1,0:T(8,128)(2,1)}), bf16[2,352,1024]{2,1,0:T(8,128)(2,1)}) %reduce-scatter.11.cloned.1.call-update) | async-done | bytes 1441808 | tf_op jit(solution)/shard_map/reduce_scatter | solution.py:142
  (216 shorter events, 25.6 us)
Async XLA Ops:
  8.0 1.6 copy-start
  8.0 4.4 copy-start.14
  8.0 53.8 %all-reduce.5.cloned.1.call-start = ((), (), s32[]{:S(2)}) async-start(), calls=%async_computation.8 | async-start | bytes 1048576 | tf_op jit(solution)/shard_map/psum | solution.py:54
  11.7 50.1 %copy-start.7 = (bf16[128,2048]{1,0:T(8,128)(2,1)S(1)}, bf16[128,2048]{1,0:T(8,128)(2,1)}, u32[]{:S(2)}) copy-start(bf16[128,2048]{1,0:T(8,128)(2,1)} %param.10) | copy-start | bytes 1572868
  11.7 51.4 %copy-start.13 = (f32[2048]{0:T(1024)S(1)}, f32[2048]{0:T(1024)}, u32[]{:S(2)}) copy-start(f32[2048]{0:T(1024)} %param.12) | copy-start | bytes 24580
  11.8 85.8 %all-gather.3.cloned.1.call-start = ((), (), s32[]{:S(2)}) async-start(), calls=%async_computation.9 | async-start | bytes 8650752 | tf_op jit(solution)/shard_map/all_gather | solution.py:50
  84.2 128.9 %all-to-all-start = ((bf16[2,32,14,2048]{3,0,2,1:T(2,128)(2,1)}), bf16[2,32,14,2048]{3,0,2,1:T(2,128)(2,1)}, u32[]{:S(2)}, u32[]{:S(2)}) async-start(bf16[2,32,14,2048]{3,0,2,1:T(2,128)(2,1)} %copy.3511), calls=%async_computation | async-start | bytes 7340032 | tf_op jit(solution)/shard_map/all_to_all | solution.py:13
  96.7 132.8 %all-gather.5.cloned.1.call-start = ((), (), s32[]{:S(2)}) async-start(), calls=%async_computation.10 | async-start | bytes 4325376 | tf_op jit(solution)/shard_map/all_gather | solution.py:51
  97.2 177.4 %reduce-scatter.5.cloned.1.call-start = ((), (), s32[]{:S(2)}) async-start(), calls=%async_computation.11 | async-start | bytes 4587520 | tf_op jit(solution)/shard_map/reduce_scatter | solution.py:84
  213.1 8.6 %copy-start.1 = (bf16[2,2,2048,352]{2,3,1,0:T(8,128)(2,1)S(1)}, bf16[2,2,2048,352]{2,3,1,0:T(8,128)(2,1)}, u32[]{:S(2)}) copy-start(bf16[2,2,2048,352]{2,3,1,0:T(8,128)(2,1)} %all-gather.3.cloned.1.call-done) | copy-start | bytes 17301508
  220.6 1.2 copy-start.16
  229.5 5.9 copy-start.8
  274.6 4.1 copy-start.4
  280.4 12.8 %copy-start.15 = (f32[128,6]{0,1:T(8,128)S(1)}, f32[128,6]{0,1:T(8,128)}, u32[]{:S(2)}) copy-start(f32[128,6]{0,1:T(8,128)} %param.14) | copy-start | bytes 9220
  282.8 36.2 %all-to-all-start.1 = ((bf16[32,2,1,14,512]{4,1,3,2,0:T(2,128)(2,1)}), bf16[32,2,1,14,512]{4,1,3,2,0:T(2,128)(2,1)S(1)}, u32[]{:S(2)}, u32[]{:S(2)}) async-start(bf16[32,2,1,14,512]{4,1,3,2,0:T(2,128)(2,1)} %copy.3576), calls=%async_computation.2 | async-start | bytes 1835008 | tf_op jit(solution)/shard_map/all_to_all | solution.py:18
  293.1 213.6 %reduce-scatter.7.cloned.1.call-start = ((), (), s32[]{:S(2)}) async-start(), calls=%async_computation.12 | async-start | bytes 4587520 | tf_op jit(solution)/shard_map/reduce_scatter | solution.py:114
  324.8 4.8 copy-start.12
  360.7 92.3 %copy-start.6 = (bf16[2,352,2048]{2,1,0:T(8,128)(2,1)S(1)}, bf16[2,352,2048]{2,1,0:T(8,128)(2,1)}, u32[]{:S(2)}) copy-start(bf16[2,352,2048]{2,1,0:T(8,128)(2,1)} %all-gather.5.cloned.1.call-done) | copy-start | bytes 8650756
  360.7 100.2 %slice-start = ((s8[5767168]{0:T(1024)(128)(4,1)}), s8[4194304]{0:T(1024)(128)(4,1)S(1)}, s32[]{:S(2)}) async-start(s8[5767168]{0:T(1024)(128)(4,1)} %bitcast.269), calls=%async_computation.15 | async-start | bytes 8388608
  453.0 7.9 %copy-start.2 = (bf16[2,32,14,2048]{3,0,2,1:T(2,128)(2,1)}, bf16[2,32,14,2048]{3,0,2,1:T(2,128)(2,1)S(1)}, u32[]{:S(2)}) copy-start(bf16[2,32,14,2048]{3,0,2,1:T(2,128)(2,1)S(1)} %all_to_all.20) | copy-start | bytes 11010052
  453.0 7.9 %slice-start.1 = ((s8[5767168]{0:T(1024)(128)(4,1)}), s8[1572864]{0:T(1024)(128)(4,1)S(1)}, s32[]{:S(2)}) async-start(s8[5767168]{0:T(1024)(128)(4,1)} %bitcast.269), calls=%async_computation.16 | async-start | bytes 3145728
  460.9 2.1 copy-start.10
  467.1 138.0 %reduce-scatter.9.cloned.1.call-start = ((), (), s32[]{:S(2)}) async-start(), calls=%async_computation.13 | async-start | bytes 8650752 | tf_op jit(solution)/shard_map/reduce_scatter | solution.py:139
  467.4 6.8 %copy-start.11 = (bf16[2,32,14,352]{3,1,2,0:T(8,128)(2,1)S(1)}, bf16[2,32,14,352]{3,1,2,0:T(8,128)(2,1)}, u32[]{:S(2)}) copy-start(bf16[2,32,14,352]{3,1,2,0:T(8,128)(2,1)} %copy-done.10) | copy-start | bytes 1892356
  484.0 1.1 copy-start.9
  484.0 170.2 %reduce-scatter.11.cloned.1.call-start = ((), (), s32[]{:S(2)}) async-start(), calls=%async_computation.14 | async-start | bytes 4325376 | tf_op jit(solution)/shard_map/reduce_scatter | solution.py:142
  506.7 3.7 copy-start.3
  514.4 47.1 %all-to-all-start.3 = ((bf16[32,2,1,14,512]{4,1,3,2,0:T(2,128)(2,1)}), bf16[32,2,1,14,512]{4,1,3,2,0:T(2,128)(2,1)S(1)}, u32[]{:S(2)}, u32[]{:S(2)}) async-start(bf16[32,2,1,14,512]{4,1,3,2,0:T(2,128)(2,1)} %copy.3643), calls=%async_computation.5 | async-start | bytes 1835008 | tf_op jit(solution)/shard_map/all_to_all | solution.py:18
  567.4 4.8 copy-start.5
Sparse Core Ops, SparseCore 0:
  11.9 49.8 all-reduce.4
  235.6 38.9 reduce-scatter.4
  467.2 39.4 reduce-scatter.6
  509.1 95.9 reduce-scatter.8
  608.0 46.0 reduce-scatter.10
Sparse Core Ops, SparseCore 1:
  14.1 83.0 all-gather.2
  98.9 109.0 all-gather.4
